TPU v7x, 32 devices: a whole 2x2x4 slice. The times are simulated.
32 devices in a mesh: groups: 2 (over y), tm: 4 (over x, core), width: 4 (over z).
Axes of the slice: x: 2, y: 2, z: 4, core: 2. Of those that a mesh axis runs over, the one named last changes fastest.
Arguments:
- video: bfloat16 [32, 12, 48, 256], P(('groups', 'tm'), None, 'width'), parts along dimension 0, may hold values from -6 to 6
- conv_w: bfloat16 [2, 3, 3, 256, 256], replicated, may hold values from -0.125 to 0.125
- depth_k: float32 [2, 16, 256], replicated, may hold values from -1.5 to 1.5
- proj_w: bfloat16 [2, 256, 256], replicated, may hold values from -0.375 to 0.375
Outputs:
- result: bfloat16 [32, 12, 48, 256], P(('groups', 'tm'), None, 'width'), parts along dimension 0
There are 2 independent parts, one for each index of `groups`. A program takes and returns all parts, laid end to end along the dimension named above; an argument that names none is the same for every part. Nothing has to cross between parts.
All inputs are finite; a program needn't handle non-finite values.
Results may differ from a plain program's by a relative error of at most 0.0058.
Values may be sent and summed in bfloat16 or wider, within the bound.
No kernel may reach another device: no remote copies, remote signals or barrier semaphores. Data moves between devices by JAX's collectives and lax.ppermute only.
A program may use at most 64 MiB of HBM per device.

v0:
```python
from functools import partial
import jax
import jax.numpy as jnp
from jax import lax
from jax.sharding import PartitionSpec as P

BLOCKS = 2


def with_halo(shard, sides, width):
    for axis, dim in sides:
        peers, length = (lax.axis_size(axis), shard.shape[dim])
        up = [(i, (i + 1) % peers) for i in range(peers - 1)]
        down = [(j, i) for i, j in up]
        last = lax.slice_in_dim(shard, length - width, length, axis=dim)
        leading = lax.slice_in_dim(shard, 0, width, axis=dim)
        before = lax.ppermute(last, axis, up)
        after = lax.ppermute(leading, axis, down)
        shard = jnp.concatenate([before, shard, after], axis=dim)
    return shard


def spatial(padded, weight):
    frames = padded.shape[0]
    rows = padded.shape[1] - 2
    cols = padded.shape[2] - 2
    chans = padded.shape[3]
    total = jnp.zeros((frames * rows * cols, chans), jnp.float32)
    for dy in range(3):
        for dx in range(3):
            piece = padded[:, dy : dy + rows, dx : dx + cols, :].reshape(-1, chans)
            total = total + jnp.dot(piece, weight[dy, dx], preferred_element_type=jnp.float32)
    return total.reshape(frames, rows, cols, chans)


def toeplitz_table(kernel):
    frames = kernel.shape[0]
    later = jnp.arange(frames, dtype=jnp.int32)[:, None]
    earlier = jnp.arange(frames, dtype=jnp.int32)[None, :]
    offset = (later - earlier) % frames
    return jnp.where((later >= earlier)[:, :, None], kernel[offset], jnp.zeros((), jnp.float32))


def temporal(kernel, proj, hidden):
    chans = hidden.shape[-1]
    table = toeplitz_table(kernel)
    values = hidden.astype(jnp.float32)
    total = jnp.einsum("tsc,sijc->tijc", table, values, precision=lax.Precision.HIGHEST)
    depth = total.astype(jnp.bfloat16)
    mixed = jnp.dot(depth.reshape(-1, chans), proj, preferred_element_type=jnp.float32)
    return mixed.reshape(hidden.shape).astype(jnp.bfloat16)


def add_branch(state, mixed):
    return (state.astype(jnp.float32) + mixed.astype(jnp.float32)).astype(jnp.bfloat16)


def shards(video, conv_w, depth_k, proj_w):
    state = video
    for block in range(BLOCKS):
        extended = with_halo(state, (("width", 2),), 1)
        extended = jnp.pad(extended, ((0, 0), (1, 1), (0, 0), (0, 0)))
        hidden = jax.nn.silu(spatial(extended, conv_w[block])).astype(jnp.bfloat16)
        mixer = partial(temporal, depth_k[block], proj_w[block])
        mixed = mixer(lax.all_to_all(hidden, "tm", split_axis=1, concat_axis=0, tiled=True))
        returned = lax.all_to_all(mixed, "tm", split_axis=0, concat_axis=1, tiled=True)
        state = add_branch(state, returned)
    return state


def solution(mesh):
    return jax.shard_map(
        shards,
        mesh=mesh,
        in_specs=(P(("groups", "tm"), None, "width", None), P(), P(), P()),
        out_specs=P(("groups", "tm"), None, "width", None),
        check_vma=False,
    )
```

profile of v0, /device:TPU:0, one launch (start us, length us, event | category | flops | bytes accessed | tf_op | source)
XLA Modules:
  0.0 109.8 jit_solution(14615664582587126943)
XLA Ops:
  0.8 5.0 %collective-permute-start = (bf16[4,12,1,256]{3,0,2,1:T(4,128)(2,1)S(1)}, bf16[4,12,1,256]{3,0,2,1:T(4,128)(2,1)S(1)}, u32[]{:S(2)}, u32[]{:S(2)}) collective-permute-start(bf16[4,12,1,256]{3,0,2,1:T(4,128)(2,1)S(1)} %get-tuple-element.25), channel_id=1, source_target_pairs={{0,1},{1,2},{2,3},{4,5},{5,6},{6,7},{8,9},{9,10},{10,11},{12,13},{... | collective-permute-start | bytes 73736 | tf_op jit(solution)/shard_map/ppermute | solution.py:17
  5.8 1.4 %collective-permute-start.1 = (bf16[4,12,1,256]{3,0,2,1:T(4,128)(2,1)S(1)}, bf16[4,12,1,256]{3,0,2,1:T(4,128)(2,1)S(1)}, u32[]{:S(2)}, u32[]{:S(2)}) collective-permute-start(bf16[4,12,1,256]{3,0,2,1:T(4,128)(2,1)S(1)} %get-tuple-element.26), channel_id=1, source_target_pairs={{1,0},{2,1},{3,2},{5,4},{6,5},{7,6},{9,8},{10,9},{11,10},{13,12},{... | collective-permute-start | bytes 73736 | tf_op jit(solution)/shard_map/ppermute | solution.py:18
  7.2 2.9 %slice_bitcast_fusion = (bf16[3,3,256,256]{3,2,1,0:T(8,128)(2,1)}, bf16[3,3,256,256]{3,2,1,0:T(8,128)(2,1)S(1)}) fusion(bf16[2,3,3,256,256]{4,3,2,1,0:T(8,128)(2,1)} %param.5), kind=kLoop, calls=%fused_computation.32 | loop fusion | bytes 4718592 | tf_op jit(solution)/shard_map/squeeze | solution.py:63
  12.3 0.8 reshape.146
  13.1 0.8 reshape.147
  14.4 0.8 reshape.149
  15.2 0.8 reshape.151
  16.3 0.8 reshape.154
  22.5 0.9 copy.38
  23.4 3.5 %all-to-all-start = ((bf16[4,12,12,256]{3,0,2,1:T(4,128)(2,1)}), bf16[4,12,12,256]{3,0,2,1:T(4,128)(2,1)S(1)}, u32[]{:S(2)}, u32[]{:S(2)}) async-start(bf16[4,12,12,256]{3,0,2,1:T(4,128)(2,1)} %copy.38), calls=%async_computation | async-start | bytes 589824 | tf_op jit(solution)/shard_map/all_to_all | solution.py:65
  26.9 1.0 gather_fusion
  27.9 2.5 %copy.40 = f32[16,16,256]{1,0,2:T(8,128)} copy(f32[16,16,256]{2,1,0:T(8,128)S(1)} %bitcast.149) | data formatting | bytes 524288 | tf_op jit(solution)/shard_map/gather | solution.py:41
  30.4 2.8 %all-to-all-done = bf16[4,12,12,256]{3,0,2,1:T(4,128)(2,1)S(1)} async-done(((bf16[4,12,12,256]{3,0,2,1:T(4,128)(2,1)}), bf16[4,12,12,256]{3,0,2,1:T(4,128)(2,1)S(1)}, u32[]{:S(2)}, u32[]{:S(2)}) %all-to-all-start) | async-done | bytes 294944 | tf_op jit(solution)/shard_map/all_to_all | solution.py:65
  33.4 2.9 %copy.41 = bf16[16,3,12,256]{0,2,1,3:T(8,128)(2,1)S(1)} copy(bf16[16,3,12,256]{3,0,2,1:T(8,128)(2,1)S(1)} %all_to_all.43) | data formatting | bytes 589824 | tf_op jit(solution)/shard_map/all_to_all | solution.py:65
  36.3 6.9 %convert_bitcast_fusion.1 = bf16[16,3,12,256]{0,2,1,3:T(8,128)(2,1)S(1)} fusion(bf16[16,3,12,256]{0,2,1,3:T(8,128)(2,1)S(1)} %copy.41, f32[16,16,256]{1,0,2:T(8,128)} %copy.40, pred[16,16]{1,0:T(8,128)(4,1)S(1)} %iota_compare_fusion.2), kind=kOutput, calls=%fused_computation.3 | convolution fusion | flops 28524544 | bytes 852224 | tf_op jit(solution)/shard_map/tsc,sijc->tijc/dot_general | solution.py:48
  44.1 9.8 %all_to_all.54 = bf16[16,3,12,256]{3,2,1,0:T(8,128)(2,1)S(1)} all-to-all(bf16[16,3,12,256]{3,2,1,0:T(8,128)(2,1)S(1)} %copy.43), channel_id=1, replica_groups=mesh['groups'=2,'tm'=4,'width'=4] {'tm'}, dimensions={0} | all-to-all | bytes 589824 | tf_op jit(solution)/shard_map/all_to_all | solution.py:66
  55.1 3.9 %collective-permute-start.2 = (bf16[4,12,1,256]{3,0,2,1:T(4,128)(2,1)S(1)}, bf16[4,12,1,256]{3,0,2,1:T(4,128)(2,1)S(1)}, u32[]{:S(2)}, u32[]{:S(2)}) collective-permute-start(bf16[4,12,1,256]{3,0,2,1:T(4,128)(2,1)S(1)} %get-tuple-element.21), channel_id=1, source_target_pairs={{0,1},{1,2},{2,3},{4,5},{5,6},{6,7},{8,9},{9,10},{10,11},{12,13},{... | collective-permute-start | bytes 73736 | tf_op jit(solution)/shard_map/ppermute | solution.py:17
  59.0 1.5 %collective-permute-start.3 = (bf16[4,12,1,256]{3,0,2,1:T(4,128)(2,1)S(1)}, bf16[4,12,1,256]{3,0,2,1:T(4,128)(2,1)S(1)}, u32[]{:S(2)}, u32[]{:S(2)}) collective-permute-start(bf16[4,12,1,256]{3,0,2,1:T(4,128)(2,1)S(1)} %get-tuple-element.22), channel_id=1, source_target_pairs={{1,0},{2,1},{3,2},{5,4},{6,5},{7,6},{9,8},{10,9},{11,10},{13,12},{... | collective-permute-start | bytes 73736 | tf_op jit(solution)/shard_map/ppermute | solution.py:18
  60.7 4.1 %collective-permute-done.3 = bf16[4,12,1,256]{3,0,2,1:T(4,128)(2,1)S(1)} collective-permute-done((bf16[4,12,1,256]{3,0,2,1:T(4,128)(2,1)S(1)}, bf16[4,12,1,256]{3,0,2,1:T(4,128)(2,1)S(1)}, u32[]{:S(2)}, u32[]{:S(2)}) %collective-permute-start.3) | collective-permute-done | bytes 24608 | tf_op jit(solution)/shard_map/ppermute | solution.py:18
  66.0 0.8 reshape.157
  68.6 0.8 reshape.163
  69.4 0.8 reshape.164
  75.4 0.9 copy.54
  76.3 3.5 %all-to-all-start.2 = ((bf16[4,12,12,256]{3,0,2,1:T(4,128)(2,1)}), bf16[4,12,12,256]{3,0,2,1:T(4,128)(2,1)S(1)}, u32[]{:S(2)}, u32[]{:S(2)}) async-start(bf16[4,12,12,256]{3,0,2,1:T(4,128)(2,1)} %copy.54), calls=%async_computation.2 | async-start | bytes 589824 | tf_op jit(solution)/shard_map/all_to_all | solution.py:65
  79.8 1.0 gather_fusion.1
  80.7 2.5 %copy.56 = f32[16,16,256]{1,0,2:T(8,128)} copy(f32[16,16,256]{2,1,0:T(8,128)S(1)} %bitcast.148) | data formatting | bytes 524288 | tf_op jit(solution)/shard_map/gather | solution.py:41
  83.2 2.9 %all-to-all-done.2 = bf16[4,12,12,256]{3,0,2,1:T(4,128)(2,1)S(1)} async-done(((bf16[4,12,12,256]{3,0,2,1:T(4,128)(2,1)}), bf16[4,12,12,256]{3,0,2,1:T(4,128)(2,1)S(1)}, u32[]{:S(2)}, u32[]{:S(2)}) %all-to-all-start.2) | async-done | bytes 294944 | tf_op jit(solution)/shard_map/all_to_all | solution.py:65
  86.2 0.8 all_to_all.48
  87.0 3.8 %copy.57 = bf16[16,3,12,256]{0,2,1,3:T(8,128)(2,1)S(1)} copy(bf16[16,3,12,256]{3,0,2,1:T(8,128)(2,1)} %all_to_all.48) | data formatting | bytes 589824 | tf_op jit(solution)/shard_map/all_to_all | solution.py:65
  90.8 6.9 %convert_bitcast_fusion = bf16[16,3,12,256]{0,2,1,3:T(8,128)(2,1)S(1)} fusion(bf16[16,3,12,256]{0,2,1,3:T(8,128)(2,1)S(1)} %copy.57, f32[16,16,256]{1,0,2:T(8,128)} %copy.56, pred[16,16]{1,0:T(8,128)(4,1)S(1)} %iota_compare_fusion.2), kind=kOutput, calls=%fused_computation.2 | convolution fusion | flops 28524544 | bytes 852224 | tf_op jit(solution)/shard_map/tsc,sijc->tijc/dot_general | solution.py:48
  98.6 9.8 %all_to_all.55 = bf16[16,3,12,256]{3,2,1,0:T(8,128)(2,1)S(1)} all-to-all(bf16[16,3,12,256]{3,2,1,0:T(8,128)(2,1)S(1)} %copy.59), channel_id=1, replica_groups=mesh['groups'=2,'tm'=4,'width'=4] {'tm'}, dimensions={0} | all-to-all | bytes 589824 | tf_op jit(solution)/shard_map/all_to_all | solution.py:66
  108.9 0.9 fusion.19
  (112 shorter events, 20.9 us)
Async XLA Ops:
  0.8 10.2 %collective-permute-start = (bf16[4,12,1,256]{3,0,2,1:T(4,128)(2,1)S(1)}, bf16[4,12,1,256]{3,0,2,1:T(4,128)(2,1)S(1)}, u32[]{:S(2)}, u32[]{:S(2)}) collective-permute-start(bf16[4,12,1,256]{3,0,2,1:T(4,128)(2,1)S(1)} %get-tuple-element.25), channel_id=1, source_target_pairs={{0,1},{1,2},{2,3},{4,5},{5,6},{6,7},{8,9},{9,10},{10,11},{12,13},{... | collective-permute-start | bytes 73736 | tf_op jit(solution)/shard_map/ppermute | solution.py:17
  5.7 4.3 %copy-start.14 = (f32[2,16,256]{2,1,0:T(8,128)S(1)}, f32[2,16,256]{2,1,0:T(8,128)}, u32[]{:S(2)}) copy-start(f32[2,16,256]{2,1,0:T(8,128)} %param.6) | copy-start | bytes 98308
  5.8 4.3 %copy-start = (bf16[4,12,12,256]{3,0,2,1:T(4,128)(2,1)S(1)}, bf16[4,12,12,256]{3,0,2,1:T(4,128)(2,1)}, u32[]{:S(2)}) copy-start(bf16[4,12,12,256]{3,0,2,1:T(4,128)(2,1)} %param.4) | copy-start | bytes 884740
  5.8 5.9 %collective-permute-start.1 = (bf16[4,12,1,256]{3,0,2,1:T(4,128)(2,1)S(1)}, bf16[4,12,1,256]{3,0,2,1:T(4,128)(2,1)S(1)}, u32[]{:S(2)}, u32[]{:S(2)}) collective-permute-start(bf16[4,12,1,256]{3,0,2,1:T(4,128)(2,1)S(1)} %get-tuple-element.26), channel_id=1, source_target_pairs={{1,0},{2,1},{3,2},{5,4},{6,5},{7,6},{9,8},{10,9},{11,10},{13,12},{... | collective-permute-start | bytes 73736 | tf_op jit(solution)/shard_map/ppermute | solution.py:18
  16.1 1.0 copy-start.4
  16.2 1.1 %copy-start.5 = (bf16[576,256]{1,0:T(8,128)(2,1)S(1)}, bf16[576,256]{1,0:T(8,128)(2,1)}, u32[]{:S(2)}) copy-start(bf16[576,256]{1,0:T(8,128)(2,1)} %reshape.147) | copy-start | bytes 884740
  17.6 1.0 copy-start.8
  18.6 1.0 copy-start.3
  19.5 1.0 copy-start.6
  21.0 1.0 copy-start.12
  23.4 9.8 %all-to-all-start = ((bf16[4,12,12,256]{3,0,2,1:T(4,128)(2,1)}), bf16[4,12,12,256]{3,0,2,1:T(4,128)(2,1)S(1)}, u32[]{:S(2)}, u32[]{:S(2)}) async-start(bf16[4,12,12,256]{3,0,2,1:T(4,128)(2,1)} %copy.38), calls=%async_computation | async-start | bytes 589824 | tf_op jit(solution)/shard_map/all_to_all | solution.py:65
  36.3 6.9 %copy-start.15 = (bf16[2,256,256]{2,1,0:T(8,128)(2,1)S(1)}, bf16[2,256,256]{2,1,0:T(8,128)(2,1)}, u32[]{:S(2)}) copy-start(bf16[2,256,256]{2,1,0:T(8,128)(2,1)} %param.7) | copy-start | bytes 786436
  53.9 1.0 copy-start.1
  55.1 5.6 %collective-permute-start.2 = (bf16[4,12,1,256]{3,0,2,1:T(4,128)(2,1)S(1)}, bf16[4,12,1,256]{3,0,2,1:T(4,128)(2,1)S(1)}, u32[]{:S(2)}, u32[]{:S(2)}) collective-permute-start(bf16[4,12,1,256]{3,0,2,1:T(4,128)(2,1)S(1)} %get-tuple-element.21), channel_id=1, source_target_pairs={{0,1},{1,2},{2,3},{4,5},{5,6},{6,7},{8,9},{9,10},{10,11},{12,13},{... | collective-permute-start | bytes 73736 | tf_op jit(solution)/shard_map/ppermute | solution.py:17
  59.0 5.7 %collective-permute-start.3 = (bf16[4,12,1,256]{3,0,2,1:T(4,128)(2,1)S(1)}, bf16[4,12,1,256]{3,0,2,1:T(4,128)(2,1)S(1)}, u32[]{:S(2)}, u32[]{:S(2)}) collective-permute-start(bf16[4,12,1,256]{3,0,2,1:T(4,128)(2,1)S(1)} %get-tuple-element.22), channel_id=1, source_target_pairs={{1,0},{2,1},{3,2},{5,4},{6,5},{7,6},{9,8},{10,9},{11,10},{13,12},{... | collective-permute-start | bytes 73736 | tf_op jit(solution)/shard_map/ppermute | solution.py:18
  68.6 1.6 %copy-start.2 = (bf16[3,3,256,256]{3,2,1,0:T(8,128)(2,1)S(1)}, bf16[3,3,256,256]{3,2,1,0:T(8,128)(2,1)}, u32[]{:S(2)}) copy-start(bf16[3,3,256,256]{3,2,1,0:T(8,128)(2,1)} %get-tuple-element.5) | copy-start | bytes 3538948
  69.4 1.1 copy-start.10
  70.2 1.0 copy-start.13
  71.9 1.0 copy-start.7
  72.9 1.0 copy-start.9
  73.9 1.0 copy-start.11
  76.3 9.8 %all-to-all-start.2 = ((bf16[4,12,12,256]{3,0,2,1:T(4,128)(2,1)}), bf16[4,12,12,256]{3,0,2,1:T(4,128)(2,1)S(1)}, u32[]{:S(2)}, u32[]{:S(2)}) async-start(bf16[4,12,12,256]{3,0,2,1:T(4,128)(2,1)} %copy.54), calls=%async_computation.2 | async-start | bytes 589824 | tf_op jit(solution)/shard_map/all_to_all | solution.py:65
  90.8 6.9 %copy-start.16 = (bf16[2,256,256]{2,1,0:T(8,128)(2,1)S(1)}, bf16[2,256,256]{2,1,0:T(8,128)(2,1)}, u32[]{:S(2)}) copy-start(bf16[2,256,256]{2,1,0:T(8,128)(2,1)} %param.7) | copy-start | bytes 786436
where the time goes:
time: 111 us; the launch traced here: 110 us
  local copies, waits for them, and re-layouts  38.4 us (35%)
  blocking collectives  19.6 us (18%)
  matrix products  19.4 us (17%)
  starting transfers between devices  18.7 us (17%)
  waiting for transfers between devices  10.4 us (9%)
  other arithmetic  2.54 us (2%)
    all_to_all x2, blocking collectives, shards(): lax.all_to_all(mixed, 'tm', split_axis=0, concat_axis=1, tiled=True)  19.6 us
    dot_general x2, matrix products, temporal(): jnp.einsum('tsc,sijc->tijc', table, values, precision=lax.Precision.HIGHEST)  13.7 us
    reshape x18, local copies, waits for them, and re-layouts, spatial(): piece = padded[:, dy:dy + rows, dx:dx + cols, :].reshape(-1, chans)  9.05 us
    ppermute x2, starting transfers between devices, with_halo(): before = lax.ppermute(last, axis, up)  8.9 us
    all_to_all x6, local copies, waits for them, and re-layouts, shards(): lax.all_to_all(hidden, 'tm', split_axis=1, concat_axis=0, tiled=True)  7.8 us
    gather x4, local copies, waits for them, and re-layouts, toeplitz_table(): kernel[offset]  6.91 us
    all_to_all x2, starting transfers between devices, shards(): lax.all_to_all(hidden, 'tm', split_axis=1, concat_axis=0, tiled=True)  6.9 us
    unnamed x35, local copies, waits for them, and re-layouts  6.14 us
  transfers between devices with their start and end apart: 6, of which 4 were waited for; matrix products, arithmetic and copies ran while one was open for 10% of the time, Pallas kernels for 0%

commit v1 on v0

--- a/solution.py
+++ b/solution.py
@@ -5,6 +5,18 @@
 from jax.sharding import PartitionSpec as P
 
 BLOCKS = 2
+
+
+def cut_along(x, dim, size):
+    shape = x.shape
+    pieces = x.reshape(*shape[:dim], size, shape[dim] // size, *shape[dim + 1 :])
+    return jnp.moveaxis(pieces, dim, 0)
+
+
+def in_order(blocks, dim):
+    dims = list(blocks.shape[1:])
+    dims[dim] *= blocks.shape[0]
+    return jnp.moveaxis(blocks, 0, dim).reshape(dims)
 
 
 def with_halo(shard, sides, width):
@@ -63,7 +75,14 @@
         hidden = jax.nn.silu(spatial(extended, conv_w[block])).astype(jnp.bfloat16)
         mixer = partial(temporal, depth_k[block], proj_w[block])
         mixed = mixer(lax.all_to_all(hidden, "tm", split_axis=1, concat_axis=0, tiled=True))
-        returned = lax.all_to_all(mixed, "tm", split_axis=0, concat_axis=1, tiled=True)
+        devices, place = (lax.axis_size("tm"), lax.axis_index("tm"))
+        pieces = cut_along(mixed, 0, devices)
+        outs = [pieces[place]]
+        for turn in range(1, devices):
+            sent = pieces[place ^ turn]
+            outs.append(lax.ppermute(sent, "tm", [(i_2, i_2 ^ turn) for i_2 in range(devices)]))
+        pieces = jnp.stack(outs)[place ^ jnp.arange(devices)]
+        returned = in_order(pieces, 1)
         state = add_branch(state, returned)
     return state
 

time: 111 us -> 107 us (0.964)
  blocking collectives: 19.6 us -> 0 us
  waiting for transfers between devices: 10.4 us -> 21 us
  starting transfers between devices: 18.7 us -> 23 us
    all_to_all x2 -> x0, blocking collectives: 19.6 us -> none  [shards(): lax.all_to_all(mixed, 'tm', split_axis=0, concat_axis=1, tiled=True)]
    ppermute x0 -> x6, waiting for transfers between devices: none -> 7.71 us  [shards(): lax.ppermute(sent, 'tm', [(i_2, i_2 ^ turn) for i_2 in range(devices)])]
    ppermute x0 -> x6, starting transfers between devices: none -> 3.84 us  [shards(): lax.ppermute(sent, 'tm', [(i_2, i_2 ^ turn) for i_2 in range(devices)])]
    all_to_all x2, waiting for transfers between devices: 5.7 us -> 9.16 us  [shards(): lax.all_to_all(hidden, 'tm', split_axis=1, concat_axis=0, tiled=True)]
    gather x0 -> x2, local copies, waits for them, and re-layouts: none -> 1.66 us  [shards(): pieces = jnp.stack(outs)[place ^ jnp.arange(devices)]]
  transfers between devices with their start and end apart: 6 -> 12, of which waited for: 4 -> 7; matrix products, arithmetic and copies ran while one was open for 10% -> 10% of each run, Pallas kernels for 0% -> 0%
where the time goes in v1:
time: 107 us; the launch traced here: 106 us
  local copies, waits for them, and re-layouts  39 us (36%)
  starting transfers between devices  23 us (21%)
  waiting for transfers between devices  21 us (20%)
  matrix products  19.4 us (18%)
  other arithmetic  2.74 us (3%)
    dot_general x2, matrix products, temporal(): jnp.einsum('tsc,sijc->tijc', table, values, precision=lax.Precision.HIGHEST)  13.7 us
    ppermute x2, starting transfers between devices, with_halo(): before = lax.ppermute(last, axis, up)  9.51 us
    all_to_all x2, waiting for transfers between devices, shards(): lax.all_to_all(hidden, 'tm', split_axis=1, concat_axis=0, tiled=True)  9.16 us
    reshape x18, local copies, waits for them, and re-layouts, spatial(): piece = padded[:, dy:dy + rows, dx:dx + cols, :].reshape(-1, chans)  9.11 us
    all_to_all x6, local copies, waits for them, and re-layouts, shards(): lax.all_to_all(hidden, 'tm', split_axis=1, concat_axis=0, tiled=True)  7.8 us
    ppermute x6, waiting for transfers between devices, shards(): lax.ppermute(sent, 'tm', [(i_2, i_2 ^ turn) for i_2 in range(devices)])  7.71 us
    gather x4, local copies, waits for them, and re-layouts, toeplitz_table(): kernel[offset]  6.9 us
    all_to_all x2, starting transfers between devices, shards(): lax.all_to_all(hidden, 'tm', split_axis=1, concat_axis=0, tiled=True)  6.9 us
  transfers between devices with their start and end apart: 12, of which 7 were waited for; matrix products, arithmetic and copies ran while one was open for 10% of the time, Pallas kernels for 0%

profile of v1, /device:TPU:0, one launch (start us, length us, event | category | flops | bytes accessed | tf_op | source)
XLA Modules:
  0.0 105.9 jit_solution(15507798509027428585)
XLA Ops:
  0.8 5.0 %collective-permute-start = (bf16[4,12,1,256]{3,0,2,1:T(4,128)(2,1)S(1)}, bf16[4,12,1,256]{3,0,2,1:T(4,128)(2,1)S(1)}, u32[]{:S(2)}, u32[]{:S(2)}) collective-permute-start(bf16[4,12,1,256]{3,0,2,1:T(4,128)(2,1)S(1)} %get-tuple-element.33), channel_id=1, source_target_pairs={{0,1},{1,2},{2,3},{4,5},{5,6},{6,7},{8,9},{9,10},{10,11},{12,13},{... | collective-permute-start | bytes 73736 | tf_op jit(solution)/shard_map/ppermute | solution.py:29
  5.7 1.3 %collective-permute-start.1 = (bf16[4,12,1,256]{3,0,2,1:T(4,128)(2,1)S(1)}, bf16[4,12,1,256]{3,0,2,1:T(4,128)(2,1)S(1)}, u32[]{:S(2)}, u32[]{:S(2)}) collective-permute-start(bf16[4,12,1,256]{3,0,2,1:T(4,128)(2,1)S(1)} %get-tuple-element.34), channel_id=1, source_target_pairs={{1,0},{2,1},{3,2},{5,4},{6,5},{7,6},{9,8},{10,9},{11,10},{13,12},{... | collective-permute-start | bytes 73736 | tf_op jit(solution)/shard_map/ppermute | solution.py:30
  7.1 2.9 %slice_bitcast_fusion = (bf16[3,3,256,256]{3,2,1,0:T(8,128)(2,1)}, bf16[3,3,256,256]{3,2,1,0:T(8,128)(2,1)S(1)}) fusion(bf16[2,3,3,256,256]{4,3,2,1,0:T(8,128)(2,1)} %param.5), kind=kLoop, calls=%fused_computation.34 | loop fusion | bytes 4718592 | tf_op jit(solution)/shard_map/squeeze | solution.py:75
  10.9 1.0 gather_fusion
  11.9 2.5 %copy.36 = f32[16,16,256]{1,0,2:T(8,128)} copy(f32[16,16,256]{2,1,0:T(8,128)S(1)} %bitcast.171) | data formatting | bytes 524288 | tf_op jit(solution)/shard_map/gather | solution.py:53
  15.9 0.8 reshape.167
  19.1 0.8 reshape.174
  25.2 0.9 copy.34
  26.2 3.5 %all-to-all-start = ((bf16[4,12,12,256]{3,0,2,1:T(4,128)(2,1)}), bf16[4,12,12,256]{3,0,2,1:T(4,128)(2,1)S(1)}, u32[]{:S(2)}, u32[]{:S(2)}) async-start(bf16[4,12,12,256]{3,0,2,1:T(4,128)(2,1)} %copy.34), calls=%async_computation | async-start | bytes 589824 | tf_op jit(solution)/shard_map/all_to_all | solution.py:77
  29.7 6.3 %all-to-all-done = bf16[4,12,12,256]{3,0,2,1:T(4,128)(2,1)S(1)} async-done(((bf16[4,12,12,256]{3,0,2,1:T(4,128)(2,1)}), bf16[4,12,12,256]{3,0,2,1:T(4,128)(2,1)S(1)}, u32[]{:S(2)}, u32[]{:S(2)}) %all-to-all-start) | async-done | bytes 294944 | tf_op jit(solution)/shard_map/all_to_all | solution.py:77
  36.2 2.9 %copy.37 = bf16[16,3,12,256]{0,2,1,3:T(8,128)(2,1)S(1)} copy(bf16[16,3,12,256]{3,0,2,1:T(8,128)(2,1)S(1)} %all_to_all.29) | data formatting | bytes 589824 | tf_op jit(solution)/shard_map/all_to_all | solution.py:77
  39.1 6.9 %convert_bitcast_fusion.1 = bf16[16,3,12,256]{0,2,1,3:T(8,128)(2,1)S(1)} fusion(bf16[16,3,12,256]{0,2,1,3:T(8,128)(2,1)S(1)} %copy.37, f32[16,16,256]{1,0,2:T(8,128)} %copy.36, pred[16,16]{1,0:T(8,128)(4,1)S(1)} %iota_compare_fusion.2), kind=kOutput, calls=%fused_computation.5 | convolution fusion | flops 28524544 | bytes 852224 | tf_op jit(solution)/shard_map/tsc,sijc->tijc/dot_general | solution.py:60
  47.5 1.4 %collective-permute-start.4 = (bf16[4,3,12,256]{3,0,2,1:T(4,128)(2,1)S(1)}, bf16[4,3,12,256]{3,0,2,1:T(4,128)(2,1)S(1)}, u32[]{:S(2)}, u32[]{:S(2)}) collective-permute-start(bf16[4,3,12,256]{3,0,2,1:T(4,128)(2,1)S(1)} %get-tuple-element.28), channel_id=1, source_target_pairs={{0,12},{4,8},{8,4},{12,0},{1,13},{5,9},{9,5},{13,1},{2,14},{6,10},... | collective-permute-start | bytes 221192 | tf_op jit(solution)/shard_map/ppermute | solution.py:83
  48.9 3.3 %collective-permute-done.3 = bf16[4,3,12,256]{3,0,2,1:T(4,128)(2,1)S(1)} collective-permute-done((bf16[4,3,12,256]{3,0,2,1:T(4,128)(2,1)S(1)}, bf16[4,3,12,256]{3,0,2,1:T(4,128)(2,1)S(1)}, u32[]{:S(2)}, u32[]{:S(2)}) %collective-permute-start.3) | collective-permute-done | bytes 73760 | tf_op jit(solution)/shard_map/ppermute | solution.py:83
  53.0 0.8 gather_fusion.1
  54.0 4.5 %collective-permute-start.5 = (bf16[4,12,1,256]{3,0,2,1:T(4,128)(2,1)S(1)}, bf16[4,12,1,256]{3,0,2,1:T(4,128)(2,1)S(1)}, u32[]{:S(2)}, u32[]{:S(2)}) collective-permute-start(bf16[4,12,1,256]{3,0,2,1:T(4,128)(2,1)S(1)} %get-tuple-element.25), channel_id=1, source_target_pairs={{0,1},{1,2},{2,3},{4,5},{5,6},{6,7},{8,9},{9,10},{10,11},{12,13},{... | collective-permute-start | bytes 73736 | tf_op jit(solution)/shard_map/ppermute | solution.py:29
  58.6 1.5 %collective-permute-start.6 = (bf16[4,12,1,256]{3,0,2,1:T(4,128)(2,1)S(1)}, bf16[4,12,1,256]{3,0,2,1:T(4,128)(2,1)S(1)}, u32[]{:S(2)}, u32[]{:S(2)}) collective-permute-start(bf16[4,12,1,256]{3,0,2,1:T(4,128)(2,1)S(1)} %get-tuple-element.26), channel_id=1, source_target_pairs={{1,0},{2,1},{3,2},{5,4},{6,5},{7,6},{9,8},{10,9},{11,10},{13,12},{... | collective-permute-start | bytes 73736 | tf_op jit(solution)/shard_map/ppermute | solution.py:30
  60.2 4.1 %collective-permute-done.6 = bf16[4,12,1,256]{3,0,2,1:T(4,128)(2,1)S(1)} collective-permute-done((bf16[4,12,1,256]{3,0,2,1:T(4,128)(2,1)S(1)}, bf16[4,12,1,256]{3,0,2,1:T(4,128)(2,1)S(1)}, u32[]{:S(2)}, u32[]{:S(2)}) %collective-permute-start.6) | collective-permute-done | bytes 24608 | tf_op jit(solution)/shard_map/ppermute | solution.py:30
  67.3 0.8 reshape.183
  68.1 0.8 reshape.184
  74.9 0.9 copy.48
  75.8 3.5 %all-to-all-start.1 = ((bf16[4,12,12,256]{3,0,2,1:T(4,128)(2,1)}), bf16[4,12,12,256]{3,0,2,1:T(4,128)(2,1)S(1)}, u32[]{:S(2)}, u32[]{:S(2)}) async-start(bf16[4,12,12,256]{3,0,2,1:T(4,128)(2,1)} %copy.48), calls=%async_computation.1 | async-start | bytes 589824 | tf_op jit(solution)/shard_map/all_to_all | solution.py:77
  79.3 1.0 gather_fusion.2
  80.3 2.5 %copy.50 = f32[16,16,256]{1,0,2:T(8,128)} copy(f32[16,16,256]{2,1,0:T(8,128)S(1)} %bitcast.170) | data formatting | bytes 524288 | tf_op jit(solution)/shard_map/gather | solution.py:53
  82.8 2.9 %all-to-all-done.1 = bf16[4,12,12,256]{3,0,2,1:T(4,128)(2,1)S(1)} async-done(((bf16[4,12,12,256]{3,0,2,1:T(4,128)(2,1)}), bf16[4,12,12,256]{3,0,2,1:T(4,128)(2,1)S(1)}, u32[]{:S(2)}, u32[]{:S(2)}) %all-to-all-start.1) | async-done | bytes 294944 | tf_op jit(solution)/shard_map/all_to_all | solution.py:77
  85.7 0.8 all_to_all.33
  86.5 3.8 %copy.51 = bf16[16,3,12,256]{0,2,1,3:T(8,128)(2,1)S(1)} copy(bf16[16,3,12,256]{3,0,2,1:T(8,128)(2,1)} %all_to_all.33) | data formatting | bytes 589824 | tf_op jit(solution)/shard_map/all_to_all | solution.py:77
  90.3 6.9 %convert_bitcast_fusion = bf16[16,3,12,256]{0,2,1,3:T(8,128)(2,1)S(1)} fusion(bf16[16,3,12,256]{0,2,1,3:T(8,128)(2,1)S(1)} %copy.51, f32[16,16,256]{1,0,2:T(8,128)} %copy.50, pred[16,16]{1,0:T(8,128)(4,1)S(1)} %iota_compare_fusion.2), kind=kOutput, calls=%fused_computation.4 | convolution fusion | flops 28524544 | bytes 852224 | tf_op jit(solution)/shard_map/tsc,sijc->tijc/dot_general | solution.py:60
  98.7 1.4 %collective-permute-start.9 = (bf16[4,3,12,256]{3,0,2,1:T(4,128)(2,1)S(1)}, bf16[4,3,12,256]{3,0,2,1:T(4,128)(2,1)S(1)}, u32[]{:S(2)}, u32[]{:S(2)}) collective-permute-start(bf16[4,3,12,256]{3,0,2,1:T(4,128)(2,1)S(1)} %get-tuple-element.20), channel_id=1, source_target_pairs={{0,12},{4,8},{8,4},{12,0},{1,13},{5,9},{9,5},{13,1},{2,14},{6,10},... | collective-permute-start | bytes 221192 | tf_op jit(solution)/shard_map/ppermute | solution.py:83
  100.1 3.4 %collective-permute-done.8 = bf16[4,3,12,256]{3,0,2,1:T(4,128)(2,1)S(1)} collective-permute-done((bf16[4,3,12,256]{3,0,2,1:T(4,128)(2,1)S(1)}, bf16[4,3,12,256]{3,0,2,1:T(4,128)(2,1)S(1)}, u32[]{:S(2)}, u32[]{:S(2)}) %collective-permute-start.8) | collective-permute-done | bytes 73760 | tf_op jit(solution)/shard_map/ppermute | solution.py:83
  104.2 0.8 gather_fusion.3
  105.0 0.9 fusion.19
  (126 shorter events, 24.6 us)
Async XLA Ops:
  0.8 13.6 %collective-permute-start = (bf16[4,12,1,256]{3,0,2,1:T(4,128)(2,1)S(1)}, bf16[4,12,1,256]{3,0,2,1:T(4,128)(2,1)S(1)}, u32[]{:S(2)}, u32[]{:S(2)}) collective-permute-start(bf16[4,12,1,256]{3,0,2,1:T(4,128)(2,1)S(1)} %get-tuple-element.33), channel_id=1, source_target_pairs={{0,1},{1,2},{2,3},{4,5},{5,6},{6,7},{8,9},{9,10},{10,11},{12,13},{... | collective-permute-start | bytes 73736 | tf_op jit(solution)/shard_map/ppermute | solution.py:29
  5.7 8.6 %collective-permute-start.1 = (bf16[4,12,1,256]{3,0,2,1:T(4,128)(2,1)S(1)}, bf16[4,12,1,256]{3,0,2,1:T(4,128)(2,1)S(1)}, u32[]{:S(2)}, u32[]{:S(2)}) collective-permute-start(bf16[4,12,1,256]{3,0,2,1:T(4,128)(2,1)S(1)} %get-tuple-element.34), channel_id=1, source_target_pairs={{1,0},{2,1},{3,2},{5,4},{6,5},{7,6},{9,8},{10,9},{11,10},{13,12},{... | collective-permute-start | bytes 73736 | tf_op jit(solution)/shard_map/ppermute | solution.py:30
  7.1 2.9 %copy-start.14 = (f32[2,16,256]{2,1,0:T(8,128)S(1)}, f32[2,16,256]{2,1,0:T(8,128)}, u32[]{:S(2)}) copy-start(f32[2,16,256]{2,1,0:T(8,128)} %param.6) | copy-start | bytes 98308
  7.1 3.0 %copy-start = (bf16[4,12,12,256]{3,0,2,1:T(4,128)(2,1)S(1)}, bf16[4,12,12,256]{3,0,2,1:T(4,128)(2,1)}, u32[]{:S(2)}) copy-start(bf16[4,12,12,256]{3,0,2,1:T(4,128)(2,1)} %param.4) | copy-start | bytes 884740
  18.9 1.0 copy-start.4
  19.0 1.1 %copy-start.5 = (bf16[576,256]{1,0:T(8,128)(2,1)S(1)}, bf16[576,256]{1,0:T(8,128)(2,1)}, u32[]{:S(2)}) copy-start(bf16[576,256]{1,0:T(8,128)(2,1)} %reshape.167) | copy-start | bytes 884740
  20.4 1.0 copy-start.8
  21.3 1.0 copy-start.3
  22.3 1.0 copy-start.6
  23.8 1.0 copy-start.12
  26.2 9.8 %all-to-all-start = ((bf16[4,12,12,256]{3,0,2,1:T(4,128)(2,1)}), bf16[4,12,12,256]{3,0,2,1:T(4,128)(2,1)S(1)}, u32[]{:S(2)}, u32[]{:S(2)}) async-start(bf16[4,12,12,256]{3,0,2,1:T(4,128)(2,1)} %copy.34), calls=%async_computation | async-start | bytes 589824 | tf_op jit(solution)/shard_map/all_to_all | solution.py:77
  39.1 6.9 %copy-start.15 = (bf16[2,256,256]{2,1,0:T(8,128)(2,1)S(1)}, bf16[2,256,256]{2,1,0:T(8,128)(2,1)}, u32[]{:S(2)}) copy-start(bf16[2,256,256]{2,1,0:T(8,128)(2,1)} %param.7) | copy-start | bytes 786436
  46.8 7.1 %copy-start.1 = (bf16[4,12,12,256]{3,0,2,1:T(4,128)(2,1)S(1)}, bf16[4,12,12,256]{3,0,2,1:T(4,128)(2,1)}, u32[]{:S(2)}) copy-start(bf16[4,12,12,256]{3,0,2,1:T(4,128)(2,1)} %param.4) | copy-start | bytes 884740
  47.0 1.9 %collective-permute-start.2 = (bf16[4,3,12,256]{3,0,2,1:T(4,128)(2,1)S(1)}, bf16[4,3,12,256]{3,0,2,1:T(4,128)(2,1)S(1)}, u32[]{:S(2)}, u32[]{:S(2)}) collective-permute-start(bf16[4,3,12,256]{3,0,2,1:T(4,128)(2,1)S(1)} %get-tuple-element.30), channel_id=1, source_target_pairs={{0,4},{4,0},{8,12},{12,8},{1,5},{5,1},{9,13},{13,9},{2,6},{6,2},{1... | collective-permute-start | bytes 221192 | tf_op jit(solution)/shard_map/ppermute | solution.py:83
  47.1 5.2 %collective-permute-start.3 = (bf16[4,3,12,256]{3,0,2,1:T(4,128)(2,1)S(1)}, bf16[4,3,12,256]{3,0,2,1:T(4,128)(2,1)S(1)}, u32[]{:S(2)}, u32[]{:S(2)}) collective-permute-start(bf16[4,3,12,256]{3,0,2,1:T(4,128)(2,1)S(1)} %get-tuple-element.29), channel_id=1, source_target_pairs={{0,8},{4,12},{8,0},{12,4},{1,9},{5,13},{9,1},{13,5},{2,10},{6,14},... | collective-permute-start | bytes 221192 | tf_op jit(solution)/shard_map/ppermute | solution.py:83
  47.5 5.3 %collective-permute-start.4 = (bf16[4,3,12,256]{3,0,2,1:T(4,128)(2,1)S(1)}, bf16[4,3,12,256]{3,0,2,1:T(4,128)(2,1)S(1)}, u32[]{:S(2)}, u32[]{:S(2)}) collective-permute-start(bf16[4,3,12,256]{3,0,2,1:T(4,128)(2,1)S(1)} %get-tuple-element.28), channel_id=1, source_target_pairs={{0,12},{4,8},{8,4},{12,0},{1,13},{5,9},{9,5},{13,1},{2,14},{6,10},... | collective-permute-start | bytes 221192 | tf_op jit(solution)/shard_map/ppermute | solution.py:83
  54.0 6.2 %collective-permute-start.5 = (bf16[4,12,1,256]{3,0,2,1:T(4,128)(2,1)S(1)}, bf16[4,12,1,256]{3,0,2,1:T(4,128)(2,1)S(1)}, u32[]{:S(2)}, u32[]{:S(2)}) collective-permute-start(bf16[4,12,1,256]{3,0,2,1:T(4,128)(2,1)S(1)} %get-tuple-element.25), channel_id=1, source_target_pairs={{0,1},{1,2},{2,3},{4,5},{5,6},{6,7},{8,9},{9,10},{10,11},{12,13},{... | collective-permute-start | bytes 73736 | tf_op jit(solution)/shard_map/ppermute | solution.py:29
  58.6 5.7 %collective-permute-start.6 = (bf16[4,12,1,256]{3,0,2,1:T(4,128)(2,1)S(1)}, bf16[4,12,1,256]{3,0,2,1:T(4,128)(2,1)S(1)}, u32[]{:S(2)}, u32[]{:S(2)}) collective-permute-start(bf16[4,12,1,256]{3,0,2,1:T(4,128)(2,1)S(1)} %get-tuple-element.26), channel_id=1, source_target_pairs={{1,0},{2,1},{3,2},{5,4},{6,5},{7,6},{9,8},{10,9},{11,10},{13,12},{... | collective-permute-start | bytes 73736 | tf_op jit(solution)/shard_map/ppermute | solution.py:30
  68.1 1.7 %copy-start.2 = (bf16[3,3,256,256]{3,2,1,0:T(8,128)(2,1)S(1)}, bf16[3,3,256,256]{3,2,1,0:T(8,128)(2,1)}, u32[]{:S(2)}) copy-start(bf16[3,3,256,256]{3,2,1,0:T(8,128)(2,1)} %get-tuple-element.5) | copy-start | bytes 3538948
  69.0 1.1 copy-start.10
  69.8 1.0 copy-start.13
  71.5 1.0 copy-start.7
  72.4 1.0 copy-start.9
  73.4 1.0 copy-start.11
  75.8 9.8 %all-to-all-start.1 = ((bf16[4,12,12,256]{3,0,2,1:T(4,128)(2,1)}), bf16[4,12,12,256]{3,0,2,1:T(4,128)(2,1)S(1)}, u32[]{:S(2)}, u32[]{:S(2)}) async-start(bf16[4,12,12,256]{3,0,2,1:T(4,128)(2,1)} %copy.48), calls=%async_computation.1 | async-start | bytes 589824 | tf_op jit(solution)/shard_map/all_to_all | solution.py:77
  90.3 6.9 %copy-start.16 = (bf16[2,256,256]{2,1,0:T(8,128)(2,1)S(1)}, bf16[2,256,256]{2,1,0:T(8,128)(2,1)}, u32[]{:S(2)}) copy-start(bf16[2,256,256]{2,1,0:T(8,128)(2,1)} %param.7) | copy-start | bytes 786436
  98.2 1.9 %collective-permute-start.7 = (bf16[4,3,12,256]{3,0,2,1:T(4,128)(2,1)S(1)}, bf16[4,3,12,256]{3,0,2,1:T(4,128)(2,1)S(1)}, u32[]{:S(2)}, u32[]{:S(2)}) collective-permute-start(bf16[4,3,12,256]{3,0,2,1:T(4,128)(2,1)S(1)} %get-tuple-element.22), channel_id=1, source_target_pairs={{0,4},{4,0},{8,12},{12,8},{1,5},{5,1},{9,13},{13,9},{2,6},{6,2},{1... | collective-permute-start | bytes 221192 | tf_op jit(solution)/shard_map/ppermute | solution.py:83
  98.3 5.2 %collective-permute-start.8 = (bf16[4,3,12,256]{3,0,2,1:T(4,128)(2,1)S(1)}, bf16[4,3,12,256]{3,0,2,1:T(4,128)(2,1)S(1)}, u32[]{:S(2)}, u32[]{:S(2)}) collective-permute-start(bf16[4,3,12,256]{3,0,2,1:T(4,128)(2,1)S(1)} %get-tuple-element.21), channel_id=1, source_target_pairs={{0,8},{4,12},{8,0},{12,4},{1,9},{5,13},{9,1},{13,5},{2,10},{6,14},... | collective-permute-start | bytes 221192 | tf_op jit(solution)/shard_map/ppermute | solution.py:83
  98.7 5.2 %collective-permute-start.9 = (bf16[4,3,12,256]{3,0,2,1:T(4,128)(2,1)S(1)}, bf16[4,3,12,256]{3,0,2,1:T(4,128)(2,1)S(1)}, u32[]{:S(2)}, u32[]{:S(2)}) collective-permute-start(bf16[4,3,12,256]{3,0,2,1:T(4,128)(2,1)S(1)} %get-tuple-element.20), channel_id=1, source_target_pairs={{0,12},{4,8},{8,4},{12,0},{1,13},{5,9},{9,5},{13,1},{2,14},{6,10},... | collective-permute-start | bytes 221192 | tf_op jit(solution)/shard_map/ppermute | solution.py:83
